TPU v7x, 256 devices: a whole 4x4x8 slice. The times are simulated.
256 devices in a mesh: grp: 8 (over x, core), cell: 32 (over y, z).
Axes of the slice: x: 4, y: 4, z: 8, core: 2. Of those that a mesh axis runs over, the one named last changes fastest.
Arguments:
- rhs: float32 [128, 2, 128, 16, 128], P('grp', None, 'cell'), may hold values from -8 to 8
- log_perm: float32 [128, 128, 16, 128], P('grp', 'cell'), may hold values from -1.5 to 1.5
- porosity: float32 [128, 128, 16, 128], P('grp', 'cell'), may hold values from 0.1 to 0.3
- saturation: float32 [128, 128, 16, 128], P('grp', 'cell'), may hold values from 0.2 to 0.8
- pressure: float32 [128, 128, 16, 128], P('grp', 'cell'), may hold values from -6 to 6
- obs_values: float32 [256], replicated, may hold values from -6 to 6
- obs_error: float32 [256], replicated, may hold values from 0.1 to 1
- noise: float32 [128, 256], replicated, may hold values from -6 to 6
- well_cell: int32 [128], replicated, may hold values from 0 to 262143
- obs_well: int32 [256], replicated, may hold values from 0 to 127
Outputs:
- increment: float32 [128, 2, 128, 16, 128], P('grp', None, 'cell')
- log_perm_post: float32 [128, 128, 16, 128], P('grp', 'cell')
- porosity_post: float32 [128, 128, 16, 128], P('grp', 'cell')
All inputs are finite; a program needn't handle non-finite values.
Results may differ from a plain program's by a relative error of at most 0.0003.
Values sent between devices are 32-bit elements; how exact they have to be, the bound alone decides.
No kernel may reach another device: no remote copies, remote signals or barrier semaphores. Data moves between devices by JAX's collectives and lax.ppermute only.
A program may use at most 128 MiB of HBM per device.

v0:
```python
import math
import jax
import jax.numpy as jnp
from jax import lax
from jax.sharding import PartitionSpec as P

KRYLOV = 4
epsilon = 1e-06
time_step = 0.1
compress = 0.5
inflation = 4.0


def with_halo(block, sides, width):
    for axis, dim in sides:
        count = lax.axis_size(axis)
        forward = [(i, i + 1) for i in range(count - 1)]
        backward = [(target, source) for source, target in forward]
        low = lax.ppermute(
            lax.slice_in_dim(block, block.shape[dim] - width, None, axis=dim), axis, forward
        )
        high = lax.ppermute(lax.slice_in_dim(block, 0, width, axis=dim), axis, backward)
        block = jnp.concatenate([low, block, high], axis=dim)
    return block


def mobility(sat_field):
    return sat_field * sat_field + 0.5 * (1.0 - sat_field) * (1.0 - sat_field)


def face_pair(perm_low, perm_high, sat_low, sat_high):
    trans = (
        2.0
        * perm_low
        * perm_high
        / (perm_low + perm_high)
        * (0.5 * (mobility(sat_low) + mobility(sat_high)))
    )
    return (trans, trans * (0.5 * (sat_low + sat_high)))


def plane_faces(perm, sat_field):
    plane_rows = perm.shape[-2]
    plane_cols = perm.shape[-1]
    keep_rows = (
        lax.broadcasted_iota(jnp.int32, (plane_rows, plane_cols), 0) < plane_rows - 1
    ).astype(jnp.float32)
    keep_cols = (
        lax.broadcasted_iota(jnp.int32, (plane_rows, plane_cols), 1) < plane_cols - 1
    ).astype(jnp.float32)
    trans_y, frac_y = face_pair(
        perm, jnp.roll(perm, -1, -2), sat_field, jnp.roll(sat_field, -1, -2)
    )
    trans_z, frac_z = face_pair(
        perm, jnp.roll(perm, -1, -1), sat_field, jnp.roll(sat_field, -1, -1)
    )
    return (trans_y * keep_rows, frac_y * keep_rows, trans_z * keep_cols, frac_z * keep_cols)


def operator(padded, second, coeffs):
    accum, trans_x, frac_x, trans_y, frac_y, trans_z, frac_z = coeffs
    first = padded[..., 1:-1, :, :]
    diff_x = padded[..., 1:, :, :] - padded[..., :-1, :, :]
    diff_y = jnp.roll(first, -1, -2) - first
    diff_z = jnp.roll(first, -1, -1) - first

    def net(coef_x, coef_y, coef_z):
        flow_x = coef_x * diff_x
        flow_y = coef_y * diff_y
        flow_z = coef_z * diff_z
        return (
            flow_x[..., :-1, :, :]
            - flow_x[..., 1:, :, :]
            + (jnp.roll(flow_y, 1, -2) - flow_y)
            + (jnp.roll(flow_z, 1, -1) - flow_z)
        )

    out_pressure = accum * (compress * first + 0.5 * second) + net(trans_x, trans_y, trans_z)
    out_water = accum * second + net(frac_x, frac_y, frac_z)
    return (out_pressure, out_water)


def least_squares(columns, beta):
    rows = [list(column) for column in columns]
    cosines = []
    sines = []
    target = [beta] + [jnp.zeros_like(beta) for column in columns]
    for jdx in range(len(rows)):
        column = rows[jdx]
        for idx in range(jdx):
            upper = cosines[idx] * column[idx] + sines[idx] * column[idx + 1]
            column[idx + 1] = -sines[idx] * column[idx] + cosines[idx] * column[idx + 1]
            column[idx] = upper
        radius = jnp.sqrt(column[jdx] * column[jdx] + column[jdx + 1] * column[jdx + 1])
        cosines.append(column[jdx] / radius)
        sines.append(column[jdx + 1] / radius)
        column[jdx] = radius
        target[jdx + 1] = -sines[jdx] * target[jdx]
        target[jdx] = cosines[jdx] * target[jdx]
    count = len(rows)
    solved = [None] * count
    for jdx in reversed(range(count)):
        partial_sum = target[jdx]
        for idx in range(jdx + 1, count):
            partial_sum = partial_sum - rows[idx][jdx] * solved[idx]
        solved[jdx] = partial_sum / rows[jdx][jdx]
    return solved


def ensemble_weights(predicted, obs_values, obs_error, noise):
    members = predicted.shape[0]
    sigma = math.sqrt(inflation) * obs_error
    center = jnp.mean(predicted, axis=0)
    spread = (predicted - center) / (math.sqrt(members - 1.0) * sigma)
    innov = (obs_values + sigma * noise - predicted) / sigma
    gram = jnp.eye(members, dtype=jnp.float32) + jnp.dot(
        spread, spread.T, precision=lax.Precision.HIGHEST, preferred_element_type=jnp.float32
    )
    cross = jnp.dot(
        spread, innov.T, precision=lax.Precision.HIGHEST, preferred_element_type=jnp.float32
    )
    factor = jnp.linalg.cholesky(gram)
    return jax.scipy.linalg.cho_solve((factor, True), cross)


def expand(values):
    return values[:, None, None, None, None]


def inner(left, right):
    return jnp.sum(left * right, axis=(1, 2, 3, 4))


def local(
    rhs, log_perm, porosity, saturation, pressure, obs_values, obs_error, noise, well_cell, obs_well
):
    local_members, slab_x, plane_rows, plane_cols = log_perm.shape
    members = noise.shape[0]
    plane = plane_rows * plane_cols
    cells_dev = slab_x * plane
    slab_index = lax.axis_index("cell")
    slab_count = lax.axis_size("cell")
    stacked = jnp.stack([log_perm, saturation], axis=1)
    rimmed = with_halo(stacked, (("cell", 2),), 1)
    perm_pad = jnp.exp(rimmed[:, 0])
    sat_pad = rimmed[:, 1]
    trans_x, frac_x = face_pair(perm_pad[:, :-1], perm_pad[:, 1:], sat_pad[:, :-1], sat_pad[:, 1:])
    face_pos = lax.broadcasted_iota(jnp.int32, (slab_x + 1, 1, 1), 0)
    keep_face = jnp.where(
        face_pos == 0,
        slab_index > 0,
        jnp.where(face_pos == slab_x, slab_index < slab_count - 1, True),
    ).astype(jnp.float32)
    trans_x = trans_x * keep_face
    frac_x = frac_x * keep_face
    trans_y, frac_y, trans_z, frac_z = plane_faces(perm_pad[:, 1:-1], saturation)
    coeffs = (porosity / time_step, trans_x, frac_x, trans_y, frac_y, trans_z, frac_z)
    columns = []
    beta = jnp.sqrt(lax.psum(inner(rhs, rhs), "cell") + epsilon)
    basis = [rhs / expand(beta)]
    for jdx in range(KRYLOV):
        vector = basis[jdx]
        padded = with_halo(vector[:, 0], (("cell", 1),), 1)
        out_pressure, out_water = operator(padded, vector[:, 1], coeffs)
        image = jnp.stack([out_pressure, out_water], 1)
        local_dots = jnp.stack([inner(basis[idx], image) for idx in range(jdx + 1)], 0)
        projected = lax.psum(local_dots, "cell")
        for idx in range(jdx + 1):
            image = image - expand(projected[idx]) * basis[idx]
        height = jnp.sqrt(lax.psum(inner(image, image), "cell") + epsilon)
        columns.append([projected[idx] for idx in range(jdx + 1)] + [height])
        basis.append(image / expand(height))
    solved = least_squares(columns, beta)
    increment = expand(solved[0]) * basis[0]
    for jdx in range(1, KRYLOV):
        increment = increment + expand(solved[jdx]) * basis[jdx]
    flat = jnp.stack([pressure + increment[:, 0], saturation + increment[:, 1]], 1).reshape(
        local_members, 2 * cells_dev
    )
    cells = jnp.take(well_cell, obs_well)
    wells = well_cell.shape[0]
    component = (jnp.arange(obs_well.shape[0], dtype=jnp.int32) >= wells).astype(jnp.int32)
    slab_row = cells // plane - slab_index * slab_x
    inside = (slab_row >= 0) & (slab_row < slab_x)
    local_cell = jnp.where(inside, slab_row * plane + cells % plane, 0)
    picked = jnp.take(flat, component * cells_dev + local_cell, axis=1) * inside.astype(jnp.float32)
    slab_pred = lax.psum(picked, "cell")
    predicted = lax.all_gather(slab_pred, "grp", axis=0, tiled=True)
    weights = ensemble_weights(predicted, obs_values, obs_error, noise)
    params = jnp.stack([log_perm, porosity], 1).reshape(local_members, 2 * cells_dev)
    offset = lax.axis_index("grp") * local_members
    scale_factor = 1.0 / math.sqrt(members - 1.0)
    scaled = params * scale_factor
    own_columns = lax.dynamic_slice_in_dim(weights, offset, local_members, 1)
    update = jnp.dot(
        own_columns.T,
        lax.all_gather(scaled, "grp", axis=0, tiled=True),
        precision=lax.Precision.HIGHEST,
        preferred_element_type=jnp.float32,
    )
    posterior = params + update
    posterior = posterior.reshape(local_members, 2, slab_x, plane_rows, plane_cols)
    return (increment, posterior[:, 0], posterior[:, 1])


def solution(mesh):
    in_specs = (
        P("grp", None, "cell", None, None),
        P("grp", "cell", None, None),
        P("grp", "cell", None, None),
        P("grp", "cell", None, None),
        P("grp", "cell", None, None),
        P(),
        P(),
        P(),
        P(),
        P(),
    )
    out_specs = (
        P("grp", None, "cell", None, None),
        P("grp", "cell", None, None),
        P("grp", "cell", None, None),
    )
    return jax.shard_map(local, mesh=mesh, in_specs=in_specs, out_specs=out_specs, check_vma=False)
```

profile of v0, /device:TPU:1, one launch (start us, length us, event | category | flops | bytes accessed | tf_op | source)
XLA Modules:
  0.0 937.8 jit_solution(11814738720340162796)
XLA Ops:
  7.2 2.0 fusion.61
  9.3 4.5 collective-permute-start
  14.0 1.3 collective-permute-start.1
  15.3 64.8 %psum.70 = f32[16]{0:T(128)S(1)} all-reduce(f32[16]{0:T(128)S(1)} %multiply_reduce_fusion.14), channel_id=1, replica_groups=mesh['grp'=8,'cell'=32] {'cell'}, use_global_device_ids=true, to_apply=%region_1.2 | all-reduce | flops 16 | bytes 128 | tf_op jit(solution)/shard_map/psum | solution.py:159
  80.3 0.7 fusion.108
  81.0 1.3 collective-permute-start.2
  82.3 4.7 collective-permute-start.3
  87.1 1.0 copy-done.22
  88.1 1.7 bitcast_multiply_fusion
  89.9 1.9 gather_fusion
  91.9 0.8 slice.516
  92.7 1.0 slice.522
  93.7 0.9 slice.402
  94.6 1.0 slice.410
  95.7 1.1 pad_maximum_fusion
  97.3 0.7 copy-done.31
  98.5 1.1 multiply_multiply_fusion.11
  99.6 1.6 fusion.100
  101.7 2.7 fusion.60
  104.4 0.6 fusion.52
  106.6 55.7 %psum.71 = f32[16]{0:T(128)S(1)} all-reduce(f32[16]{0:T(128)S(1)} %multiply_reduce_fusion.13), channel_id=1, replica_groups=mesh['grp'=8,'cell'=32] {'cell'}, use_global_device_ids=true, to_apply=%region_3.4 | all-reduce | flops 16 | bytes 128 | tf_op jit(solution)/shard_map/psum | solution.py:167
  162.3 1.6 multiply_reduce_fusion.12
  163.9 57.9 %psum.72 = f32[16]{0:T(128)S(1)} all-reduce(f32[16]{0:T(128)S(1)} %get-tuple-element.23), channel_id=1, replica_groups=mesh['grp'=8,'cell'=32] {'cell'}, use_global_device_ids=true, to_apply=%region_5.6 | all-reduce | flops 16 | bytes 128 | tf_op jit(solution)/shard_map/psum | solution.py:170
  222.3 1.4 collective-permute-start.4
  223.7 4.0 collective-permute-start.5
  227.8 0.6 multiply_multiply_fusion.10
  228.8 0.8 collective-permute-done.5
  229.8 0.5 fusion.40
  230.4 0.6 fusion.44
  232.0 57.7 %psum.73 = f32[2,16]{1,0:T(2,128)S(1)} all-reduce(f32[2,16]{1,0:T(2,128)S(1)} %pad_maximum_fusion.14), channel_id=1, replica_groups=mesh['grp'=8,'cell'=32] {'cell'}, use_global_device_ids=true, to_apply=%region_8.9 | all-reduce | flops 32 | bytes 256 | tf_op jit(solution)/shard_map/psum | solution.py:167
  289.7 1.7 multiply_reduce_fusion.9
  291.4 55.7 %psum.74 = f32[16]{0:T(128)S(1)} all-reduce(f32[16]{0:T(128)S(1)} %get-tuple-element.21), channel_id=1, replica_groups=mesh['grp'=8,'cell'=32] {'cell'}, use_global_device_ids=true, to_apply=%region_10.11 | all-reduce | flops 16 | bytes 128 | tf_op jit(solution)/shard_map/psum | solution.py:170
  347.6 1.4 collective-permute-start.6
  349.0 4.2 collective-permute-start.7
  353.2 0.6 multiply_multiply_fusion.9
  354.4 0.6 collective-permute-done.7
  356.0 0.6 fusion.36
  356.8 0.6 multiply_reduce_fusion.8
  357.6 57.3 %psum.75 = f32[3,16]{1,0:T(4,128)S(1)} all-reduce(f32[3,16]{1,0:T(4,128)S(1)} %pad_maximum_fusion.12), channel_id=1, replica_groups=mesh['grp'=8,'cell'=32] {'cell'}, use_global_device_ids=true, to_apply=%region_14.15 | all-reduce | flops 48 | bytes 384 | tf_op jit(solution)/shard_map/psum | solution.py:167
  414.9 2.7 multiply_reduce_fusion.5
  417.6 56.2 %psum.76 = f32[16]{0:T(128)S(1)} all-reduce(f32[16]{0:T(128)S(1)} %get-tuple-element.19), channel_id=1, replica_groups=mesh['grp'=8,'cell'=32] {'cell'}, use_global_device_ids=true, to_apply=%region_16.17 | all-reduce | flops 16 | bytes 128 | tf_op jit(solution)/shard_map/psum | solution.py:170
  473.8 1.4 copy_divide_fusion
  475.6 1.4 collective-permute-start.8
  477.0 4.1 collective-permute-start.9
  481.2 0.6 multiply_multiply_fusion.8
  482.3 0.8 collective-permute-done.9
  483.5 0.5 fusion.28
  484.8 0.6 copy-done.8
  485.4 0.7 multiply_reduce_fusion.4
  486.2 57.4 %psum.77 = f32[4,16]{1,0:T(4,128)S(1)} all-reduce(f32[4,16]{1,0:T(4,128)S(1)} %pad_maximum_fusion.13), channel_id=1, replica_groups=mesh['grp'=8,'cell'=32] {'cell'}, use_global_device_ids=true, to_apply=%region_21.22 | all-reduce | flops 64 | bytes 512 | tf_op jit(solution)/shard_map/psum | solution.py:167
  543.6 2.2 multiply_reduce_fusion
  545.8 56.0 %psum.78 = f32[16]{0:T(128)S(1)} all-reduce(f32[16]{0:T(128)S(1)} %multiply_reduce_fusion), channel_id=1, replica_groups=mesh['grp'=8,'cell'=32] {'cell'}, use_global_device_ids=true, to_apply=%region_23.24 | all-reduce | flops 16 | bytes 128 | tf_op jit(solution)/shard_map/psum | solution.py:170
  602.0 1.8 multiply_add_fusion
  604.0 0.8 copy-done.43
  604.9 4.6 copy.101
  609.5 4.1 gather_fusion.1
  613.8 111.5 %psum.79 = f32[16,256]{0,1:T(8,128)S(1)} all-reduce(f32[16,256]{0,1:T(8,128)S(1)} %multiply_bitcast_fusion), channel_id=1, replica_groups=mesh['grp'=8,'cell'=32] {'cell'}, use_global_device_ids=true, to_apply=%region_24.25 | all-reduce | flops 4096 | bytes 32768 | tf_op jit(solution)/shard_map/psum | solution.py:187
  725.3 173.0 %all_gather.6 = f32[128,256]{1,0:T(8,128)S(1)} all-gather(f32[16,256]{1,0:T(8,128)S(1)} %copy.102), channel_id=1, replica_groups=mesh['grp'=8,'cell'=32] {'grp'}, dimensions={0}, use_global_device_ids=true | all-gather | bytes 147456 | tf_op jit(solution)/shard_map/all_gather | solution.py:188
  898.8 11.7 %cholesky.17 = f32[128,128]{1,0:T(8,128)S(1)} custom-call(f32[128,128]{1,0:T(8,128)S(1)} %fusion.78), custom_call_target="Cholesky" | custom-call | tf_op jit(solution)/shard_map/jit(cholesky)/cholesky | solution.py:122
  910.5 0.6 compare_reduce_fusion
  911.2 0.7 fusion.72
  911.8 9.8 %custom-call.10 = f32[1,128,128]{1,2,0:T(8,128)S(1)} custom-call(f32[1,128,128]{2,1,0:T(8,128)S(1)} %fusion.72), custom_call_target="InvertDiagBlocksLowerTriangular" | custom-call | tf_op jit(solution)/shard_map/jit(_cho_solve)/triangular_solve | solution.py:123
  922.6 7.1 fusion
  929.9 1.1 slice_bitcast_fusion.1
  (188 shorter events, 12.4 us)
Async XLA Ops:
  7.2 82.7 %copy-start = (s32[128]{0:T(128)S(1)}, s32[128]{0:T(128)}, u32[]{:S(2)}) copy-start(s32[128]{0:T(128)} %param.18) | copy-start | bytes 1540
  7.2 6.6 copy-start.2
  7.2 915.4 %all-gather.2.cloned.1.call-start = ((), (), s32[]{:S(2)}) async-start(), calls=%async_computation | async-start | bytes 9437184 | tf_op jit(solution)/shard_map/all_gather | solution.py:197
  9.3 77.7 %copy-start.5 = (f32[16,4,16,128]{3,2,1,0:T(8,128)S(1)}, f32[16,4,16,128]{3,2,1,0:T(8,128)}, u32[]{:S(2)}) copy-start(f32[16,4,16,128]{3,2,1,0:T(8,128)} %param.12) | copy-start | bytes 1572868
  9.3 77.7 %copy-start.37 = (f32[16,4,16,128]{3,2,1,0:T(8,128)S(1)}, f32[16,4,16,128]{3,2,1,0:T(8,128)}, u32[]{:S(2)}) copy-start(f32[16,4,16,128]{3,2,1,0:T(8,128)} %param.11) | copy-start | bytes 1572868
  9.3 86.4 %collective-permute-start = (f32[16,2,1,16,128]{4,3,2,0,1:T(8,128)}, f32[16,2,1,16,128]{4,3,2,0,1:T(8,128)S(1)}, u32[]{:S(2)}, u32[]{:S(2)}) collective-permute-start(f32[16,2,1,16,128]{4,3,2,0,1:T(8,128)} %get-tuple-element.67), channel_id=1, source_target_pairs={{0,1},{1,2},{2,3},{3,4},{4,5},{5,6},{6,7},{7,8},{8,9},{9,10},{10,1... | collective-permute-start | bytes 786440 | tf_op jit(solution)/shard_map/ppermute | solution.py:19
  14.0 81.7 %collective-permute-start.1 = (f32[16,2,1,16,128]{4,3,2,0,1:T(8,128)}, f32[16,2,1,16,128]{4,3,2,0,1:T(8,128)}, u32[]{:S(2)}, u32[]{:S(2)}) collective-permute-start(f32[16,2,1,16,128]{4,3,2,0,1:T(8,128)} %get-tuple-element.68), channel_id=1, source_target_pairs={{1,0},{2,1},{3,2},{4,3},{5,4},{6,5},{7,6},{8,7},{9,8},{10,9},{11,1... | collective-permute-start | bytes 786440 | tf_op jit(solution)/shard_map/ppermute | solution.py:22
  81.0 20.7 %collective-permute-start.2 = (f32[16,1,16,128]{3,2,1,0:T(8,128)}, f32[16,1,16,128]{3,2,1,0:T(8,128)}, u32[]{:S(2)}, u32[]{:S(2)}) collective-permute-start(f32[16,1,16,128]{3,2,1,0:T(8,128)} %get-tuple-element.81), channel_id=1, source_target_pairs={{1,0},{2,1},{3,2},{4,3},{5,4},{6,5},{7,6},{8,7},{9,8},{10,9},{11,1... | collective-permute-start | bytes 393224 | tf_op jit(solution)/shard_map/ppermute | solution.py:22
  82.3 19.4 %collective-permute-start.3 = (f32[16,1,16,128]{3,2,1,0:T(8,128)}, f32[16,1,16,128]{3,2,1,0:T(8,128)}, u32[]{:S(2)}, u32[]{:S(2)}) collective-permute-start(f32[16,1,16,128]{3,2,1,0:T(8,128)} %get-tuple-element.82), channel_id=1, source_target_pairs={{0,1},{1,2},{2,3},{3,4},{4,5},{5,6},{6,7},{7,8},{8,9},{9,10},{10,1... | collective-permute-start | bytes 393224 | tf_op jit(solution)/shard_map/ppermute | solution.py:19
  87.1 1.0 copy-start.22
  88.1 1.8 copy-start.45
  89.9 3.8 copy-start.3
  92.7 2.9 copy-start.46
  96.9 1.0 copy-start.31
  96.9 1.2 copy-start.32
  97.0 1.3 copy-start.33
  97.0 1.5 copy-start.34
  99.6 1.6 copy-start.12
  99.6 128.1 %copy-start.9 = (f32[16,4,16,128]{3,2,1,0:T(8,128)}, f32[16,4,16,128]{3,2,1,0:T(8,128)S(1)}, u32[]{:S(2)}) copy-start(f32[16,4,16,128]{3,2,1,0:T(8,128)S(1)} %get-tuple-element.26) | copy-start | bytes 1572868
  105.0 0.8 copy-start.35
  105.8 0.8 copy-start.36
  221.9 5.8 copy-start.13
  222.0 5.8 copy-start.24
  222.0 5.8 copy-start.27
  222.3 6.5 collective-permute-start.4
  223.7 5.9 collective-permute-start.5
  228.3 1.3 copy-start.16
  228.3 1.3 copy-start.19
  230.4 0.8 copy-start.41
  231.2 0.8 copy-start.42
  347.2 6.0 copy-start.10
  347.2 6.0 copy-start.14
  347.2 6.0 copy-start.25
  347.2 6.0 copy-start.28
  347.6 6.8 collective-permute-start.6
  349.0 6.0 collective-permute-start.7
  353.9 1.1 copy-start.17
  353.9 1.3 copy-start.20
  354.4 1.1 copy-start.6
  356.0 0.8 copy-start.39
  356.8 0.8 copy-start.40
  475.3 5.9 copy-start.11
  475.3 5.9 copy-start.15
  475.3 5.9 copy-start.26
  475.3 5.9 copy-start.29
  475.6 6.7 collective-permute-start.8
  477.0 6.1 collective-permute-start.9
  481.8 1.3 copy-start.18
  481.8 1.3 copy-start.21
  482.3 1.1 copy-start.7
  484.0 0.8 copy-start.38
  484.0 1.4 copy-start.8
  485.4 0.8 copy-start.30
  601.9 1.8 copy-start.4
  601.9 1.8 copy-start.44
  603.8 1.0 copy-start.43
  609.5 312.2 %copy-start.47 = (f32[128,256]{1,0:T(8,128)S(1)}, f32[128,256]{1,0:T(8,128)}, u32[]{:S(2)}) copy-start(f32[128,256]{1,0:T(8,128)} %param.17) | copy-start | bytes 393220
  609.5 312.2 %copy-start.48 = (f32[256]{0:T(256)S(1)}, f32[256]{0:T(256)}, u32[]{:S(2)}) copy-start(f32[256]{0:T(256)} %param.15) | copy-start | bytes 3076
  613.8 308.8 %copy-start.23 = (f32[16,2,4,16,128]{4,3,2,1,0:T(8,128)S(1)}, f32[16,2,4,16,128]{4,3,2,1,0:T(8,128)}, u32[]{:S(2)}) copy-start(f32[16,2,4,16,128]{4,3,2,1,0:T(8,128)} %copy-done.22) | copy-start | bytes 3145732
  929.7 1.3 copy-start.1
Sparse Core Ops, SparseCore 0:
  89.9 61.6 all-gather.1
where the time goes:
time: 939 us; the launch traced here: 938 us
  blocking collectives  803 us (86%)
  other arithmetic  54.4 us (6%)
  starting transfers between devices  28.3 us (3%)
  local copies, waits for them, and re-layouts  26.2 us (3%)
  between operations  15.2 us (2%)
    psum x4, blocking collectives, local(): projected = lax.psum(local_dots, 'cell')  228 us
    psum x4, blocking collectives, local(): height = jnp.sqrt(lax.psum(inner(image, image), 'cell') + epsilon)  226 us
    all_gather x1, blocking collectives, local(): predicted = lax.all_gather(slab_pred, 'grp', axis=0, tiled=True)  173 us
    psum x1, blocking collectives, local(): slab_pred = lax.psum(picked, 'cell')  111 us
    psum x1, blocking collectives, local(): beta = jnp.sqrt(lax.psum(inner(rhs, rhs), 'cell') + epsilon)  64.8 us
    ppermute x5, starting transfers between devices, with_halo(): lax.ppermute(lax.slice_in_dim(block, block.shape[dim] - width, None, axis...  21.5 us
  transfers between devices with their start and end apart: 11, of which 3 were waited for; matrix products, arithmetic and copies ran while one was open for 8% of the time, Pallas kernels for 0%

commit v1 on v0

--- a/solution.py
+++ b/solution.py
@@ -184,7 +184,7 @@
     inside = (slab_row >= 0) & (slab_row < slab_x)
     local_cell = jnp.where(inside, slab_row * plane + cells % plane, 0)
     picked = jnp.take(flat, component * cells_dev + local_cell, axis=1) * inside.astype(jnp.float32)
-    slab_pred = lax.psum(picked, "cell")
+    slab_pred = jnp.sum(lax.all_gather(picked, "cell"), axis=0)
     predicted = lax.all_gather(slab_pred, "grp", axis=0, tiled=True)
     weights = ensemble_weights(predicted, obs_values, obs_error, noise)
     params = jnp.stack([log_perm, porosity], 1).reshape(local_members, 2 * cells_dev)

time: 939 us -> 847 us (0.902)
  blocking collectives: 803 us -> 712 us
    psum x1 -> x0, blocking collectives: 111 us -> none  [local(): slab_pred = lax.psum(picked, 'cell')]
    all_gather x0 -> x1, blocking collectives: none -> 36.3 us  [local(): slab_pred = jnp.sum(lax.all_gather(picked, 'cell'), axis=0)]
    all_gather x1, blocking collectives: 173 us -> 157 us  [local(): predicted = lax.all_gather(slab_pred, 'grp', axis=0, tiled=True)]
  transfers between devices with their start and end apart: 11 -> 11, of which waited for: 3 -> 3; matrix products, arithmetic and copies ran while one was open for 8% -> 9% of each run, Pallas kernels for 0% -> 0%
where the time goes in v1:
time: 847 us; the launch traced here: 846 us
  blocking collectives  712 us (84%)
  other arithmetic  54.3 us (6%)
  starting transfers between devices  28.3 us (3%)
  local copies, waits for them, and re-layouts  26.2 us (3%)
  between operations  15.2 us (2%)
    psum x4, blocking collectives, local(): projected = lax.psum(local_dots, 'cell')  228 us
    psum x4, blocking collectives, local(): height = jnp.sqrt(lax.psum(inner(image, image), 'cell') + epsilon)  226 us
    all_gather x1, blocking collectives, local(): predicted = lax.all_gather(slab_pred, 'grp', axis=0, tiled=True)  157 us
    psum x1, blocking collectives, local(): beta = jnp.sqrt(lax.psum(inner(rhs, rhs), 'cell') + epsilon)  64.8 us
    all_gather x1, blocking collectives, local(): slab_pred = jnp.sum(lax.all_gather(picked, 'cell'), axis=0)  36.3 us
    ppermute x5, starting transfers between devices, with_halo(): lax.ppermute(lax.slice_in_dim(block, block.shape[dim] - width, None, axis...  21.5 us
  transfers between devices with their start and end apart: 11, of which 3 were waited for; matrix products, arithmetic and copies ran while one was open for 9% of the time, Pallas kernels for 0%

profile of v1, /device:TPU:1, one launch (start us, length us, event | category | flops | bytes accessed | tf_op | source)
XLA Modules:
  0.0 846.2 jit_solution(4321830589068722195)
XLA Ops:
  7.2 2.0 fusion.61
  9.3 4.5 collective-permute-start
  14.0 1.3 collective-permute-start.1
  15.3 64.8 %psum.63 = f32[16]{0:T(128)S(1)} all-reduce(f32[16]{0:T(128)S(1)} %multiply_reduce_fusion.14), channel_id=1, replica_groups=mesh['grp'=8,'cell'=32] {'cell'}, use_global_device_ids=true, to_apply=%region_1.2 | all-reduce | flops 16 | bytes 128 | tf_op jit(solution)/shard_map/psum | solution.py:159
  80.3 0.7 fusion.109
  81.0 1.3 collective-permute-start.2
  82.3 4.7 collective-permute-start.3
  87.1 1.0 copy-done.22
  88.1 1.7 bitcast_multiply_fusion
  89.9 1.9 gather_fusion
  91.9 0.8 slice.516
  92.7 1.0 slice.522
  93.7 0.9 slice.402
  94.6 1.0 slice.410
  95.7 1.1 pad_maximum_fusion
  97.3 0.7 copy-done.31
  98.5 1.1 multiply_multiply_fusion.11
  99.6 1.6 fusion.101
  101.7 2.7 fusion.60
  104.4 0.6 fusion.52
  106.5 55.7 %psum.64 = f32[16]{0:T(128)S(1)} all-reduce(f32[16]{0:T(128)S(1)} %multiply_reduce_fusion.13), channel_id=1, replica_groups=mesh['grp'=8,'cell'=32] {'cell'}, use_global_device_ids=true, to_apply=%region_3.4 | all-reduce | flops 16 | bytes 128 | tf_op jit(solution)/shard_map/psum | solution.py:167
  162.3 1.6 multiply_reduce_fusion.12
  163.9 57.9 %psum.65 = f32[16]{0:T(128)S(1)} all-reduce(f32[16]{0:T(128)S(1)} %get-tuple-element.23), channel_id=1, replica_groups=mesh['grp'=8,'cell'=32] {'cell'}, use_global_device_ids=true, to_apply=%region_5.6 | all-reduce | flops 16 | bytes 128 | tf_op jit(solution)/shard_map/psum | solution.py:170
  222.3 1.4 collective-permute-start.4
  223.7 4.0 collective-permute-start.5
  227.7 0.6 multiply_multiply_fusion.10
  228.8 0.8 collective-permute-done.5
  229.8 0.5 fusion.40
  230.4 0.6 fusion.44
  232.0 57.7 %psum.66 = f32[2,16]{1,0:T(2,128)S(1)} all-reduce(f32[2,16]{1,0:T(2,128)S(1)} %pad_maximum_fusion.14), channel_id=1, replica_groups=mesh['grp'=8,'cell'=32] {'cell'}, use_global_device_ids=true, to_apply=%region_8.9 | all-reduce | flops 32 | bytes 256 | tf_op jit(solution)/shard_map/psum | solution.py:167
  289.7 1.7 multiply_reduce_fusion.9
  291.4 55.7 %psum.67 = f32[16]{0:T(128)S(1)} all-reduce(f32[16]{0:T(128)S(1)} %get-tuple-element.21), channel_id=1, replica_groups=mesh['grp'=8,'cell'=32] {'cell'}, use_global_device_ids=true, to_apply=%region_10.11 | all-reduce | flops 16 | bytes 128 | tf_op jit(solution)/shard_map/psum | solution.py:170
  347.6 1.4 collective-permute-start.6
  349.0 4.2 collective-permute-start.7
  353.2 0.6 multiply_multiply_fusion.9
  354.4 0.6 collective-permute-done.7
  356.0 0.6 fusion.36
  356.8 0.6 multiply_reduce_fusion.8
  357.6 57.3 %psum.68 = f32[3,16]{1,0:T(4,128)S(1)} all-reduce(f32[3,16]{1,0:T(4,128)S(1)} %pad_maximum_fusion.12), channel_id=1, replica_groups=mesh['grp'=8,'cell'=32] {'cell'}, use_global_device_ids=true, to_apply=%region_14.15 | all-reduce | flops 48 | bytes 384 | tf_op jit(solution)/shard_map/psum | solution.py:167
  414.9 2.7 multiply_reduce_fusion.5
  417.6 56.2 %psum.69 = f32[16]{0:T(128)S(1)} all-reduce(f32[16]{0:T(128)S(1)} %get-tuple-element.19), channel_id=1, replica_groups=mesh['grp'=8,'cell'=32] {'cell'}, use_global_device_ids=true, to_apply=%region_16.17 | all-reduce | flops 16 | bytes 128 | tf_op jit(solution)/shard_map/psum | solution.py:170
  473.8 1.4 copy_divide_fusion
  475.6 1.4 collective-permute-start.8
  477.0 4.1 collective-permute-start.9
  481.2 0.6 multiply_multiply_fusion.8
  482.3 0.8 collective-permute-done.9
  483.4 0.5 fusion.28
  484.8 0.6 copy-done.8
  485.4 0.7 multiply_reduce_fusion.4
  486.2 57.4 %psum.70 = f32[4,16]{1,0:T(4,128)S(1)} all-reduce(f32[4,16]{1,0:T(4,128)S(1)} %pad_maximum_fusion.13), channel_id=1, replica_groups=mesh['grp'=8,'cell'=32] {'cell'}, use_global_device_ids=true, to_apply=%region_21.22 | all-reduce | flops 64 | bytes 512 | tf_op jit(solution)/shard_map/psum | solution.py:167
  543.6 2.2 multiply_reduce_fusion
  545.8 56.0 %psum.71 = f32[16]{0:T(128)S(1)} all-reduce(f32[16]{0:T(128)S(1)} %multiply_reduce_fusion), channel_id=1, replica_groups=mesh['grp'=8,'cell'=32] {'cell'}, use_global_device_ids=true, to_apply=%region_23.24 | all-reduce | flops 16 | bytes 128 | tf_op jit(solution)/shard_map/psum | solution.py:170
  601.9 1.8 multiply_add_fusion
  603.9 0.8 copy-done.43
  604.9 4.6 copy.165
  609.5 4.1 gather_fusion.1
  613.7 36.3 %all_gather.10 = f32[32,16,256]{2,1,0:T(8,128)S(1)} all-gather(f32[1,16,256]{2,1,0:T(8,128)S(1)} %fusion.85), channel_id=1, replica_groups=mesh['grp'=8,'cell'=32] {'cell'}, dimensions={0}, use_global_device_ids=true | all-gather | bytes 540672 | tf_op jit(solution)/shard_map/all_gather | solution.py:187
  650.1 156.6 %all_gather.11 = f32[128,256]{1,0:T(8,128)S(1)} all-gather(f32[16,256]{1,0:T(8,128)S(1)} %reduce_sum.168), channel_id=1, replica_groups=mesh['grp'=8,'cell'=32] {'grp'}, dimensions={0}, use_global_device_ids=true | all-gather | bytes 147456 | tf_op jit(solution)/shard_map/all_gather | solution.py:188
  807.1 11.7 %cholesky.17 = f32[128,128]{1,0:T(8,128)S(1)} custom-call(f32[128,128]{1,0:T(8,128)S(1)} %fusion.78), custom_call_target="Cholesky" | custom-call | tf_op jit(solution)/shard_map/jit(cholesky)/cholesky | solution.py:122
  818.9 0.6 compare_reduce_fusion
  819.5 0.7 fusion.72
  820.2 9.8 %custom-call.10 = f32[1,128,128]{1,2,0:T(8,128)S(1)} custom-call(f32[1,128,128]{2,1,0:T(8,128)S(1)} %fusion.72), custom_call_target="InvertDiagBlocksLowerTriangular" | custom-call | tf_op jit(solution)/shard_map/jit(_cho_solve)/triangular_solve | solution.py:123
  831.0 7.1 fusion
  838.3 1.1 slice_bitcast_fusion.1
  (189 shorter events, 12.3 us)
Async XLA Ops:
  7.2 82.7 %copy-start = (s32[128]{0:T(128)S(1)}, s32[128]{0:T(128)}, u32[]{:S(2)}) copy-start(s32[128]{0:T(128)} %param.18) | copy-start | bytes 1540
  7.2 6.6 copy-start.2
  7.2 823.7 %all-gather.2.cloned.1.call-start = ((), (), s32[]{:S(2)}) async-start(), calls=%async_computation | async-start | bytes 9437184 | tf_op jit(solution)/shard_map/all_gather | solution.py:197
  9.3 77.7 %copy-start.5 = (f32[16,4,16,128]{3,2,1,0:T(8,128)S(1)}, f32[16,4,16,128]{3,2,1,0:T(8,128)}, u32[]{:S(2)}) copy-start(f32[16,4,16,128]{3,2,1,0:T(8,128)} %param.12) | copy-start | bytes 1572868
  9.3 77.7 %copy-start.37 = (f32[16,4,16,128]{3,2,1,0:T(8,128)S(1)}, f32[16,4,16,128]{3,2,1,0:T(8,128)}, u32[]{:S(2)}) copy-start(f32[16,4,16,128]{3,2,1,0:T(8,128)} %param.11) | copy-start | bytes 1572868
  9.3 86.4 %collective-permute-start = (f32[16,2,1,16,128]{4,3,2,0,1:T(8,128)}, f32[16,2,1,16,128]{4,3,2,0,1:T(8,128)S(1)}, u32[]{:S(2)}, u32[]{:S(2)}) collective-permute-start(f32[16,2,1,16,128]{4,3,2,0,1:T(8,128)} %get-tuple-element.67), channel_id=1, source_target_pairs={{0,1},{1,2},{2,3},{3,4},{4,5},{5,6},{6,7},{7,8},{8,9},{9,10},{10,1... | collective-permute-start | bytes 786440 | tf_op jit(solution)/shard_map/ppermute | solution.py:19
  14.0 81.7 %collective-permute-start.1 = (f32[16,2,1,16,128]{4,3,2,0,1:T(8,128)}, f32[16,2,1,16,128]{4,3,2,0,1:T(8,128)}, u32[]{:S(2)}, u32[]{:S(2)}) collective-permute-start(f32[16,2,1,16,128]{4,3,2,0,1:T(8,128)} %get-tuple-element.68), channel_id=1, source_target_pairs={{1,0},{2,1},{3,2},{4,3},{5,4},{6,5},{7,6},{8,7},{9,8},{10,9},{11,1... | collective-permute-start | bytes 786440 | tf_op jit(solution)/shard_map/ppermute | solution.py:22
  81.0 20.7 %collective-permute-start.2 = (f32[16,1,16,128]{3,2,1,0:T(8,128)}, f32[16,1,16,128]{3,2,1,0:T(8,128)}, u32[]{:S(2)}, u32[]{:S(2)}) collective-permute-start(f32[16,1,16,128]{3,2,1,0:T(8,128)} %get-tuple-element.81), channel_id=1, source_target_pairs={{1,0},{2,1},{3,2},{4,3},{5,4},{6,5},{7,6},{8,7},{9,8},{10,9},{11,1... | collective-permute-start | bytes 393224 | tf_op jit(solution)/shard_map/ppermute | solution.py:22
  82.3 19.4 %collective-permute-start.3 = (f32[16,1,16,128]{3,2,1,0:T(8,128)}, f32[16,1,16,128]{3,2,1,0:T(8,128)}, u32[]{:S(2)}, u32[]{:S(2)}) collective-permute-start(f32[16,1,16,128]{3,2,1,0:T(8,128)} %get-tuple-element.82), channel_id=1, source_target_pairs={{0,1},{1,2},{2,3},{3,4},{4,5},{5,6},{6,7},{7,8},{8,9},{9,10},{10,1... | collective-permute-start | bytes 393224 | tf_op jit(solution)/shard_map/ppermute | solution.py:19
  87.1 1.0 copy-start.22
  88.1 1.8 copy-start.45
  89.9 3.8 copy-start.3
  92.7 2.9 copy-start.46
  96.9 1.0 copy-start.31
  96.9 1.2 copy-start.32
  97.0 1.3 copy-start.33
  97.0 1.5 copy-start.34
  99.6 1.6 copy-start.12
  99.6 128.1 %copy-start.9 = (f32[16,4,16,128]{3,2,1,0:T(8,128)}, f32[16,4,16,128]{3,2,1,0:T(8,128)S(1)}, u32[]{:S(2)}) copy-start(f32[16,4,16,128]{3,2,1,0:T(8,128)S(1)} %get-tuple-element.26) | copy-start | bytes 1572868
  104.9 0.8 copy-start.35
  105.7 0.8 copy-start.36
  221.9 5.8 copy-start.13
  221.9 5.8 copy-start.24
  221.9 5.8 copy-start.27
  222.3 6.5 collective-permute-start.4
  223.7 5.9 collective-permute-start.5
  228.3 1.3 copy-start.16
  228.3 1.3 copy-start.19
  230.4 0.8 copy-start.41
  231.2 0.8 copy-start.42
  347.2 6.0 copy-start.10
  347.2 6.0 copy-start.14
  347.2 6.0 copy-start.25
  347.2 6.0 copy-start.28
  347.6 6.8 collective-permute-start.6
  349.0 6.0 collective-permute-start.7
  353.8 1.1 copy-start.17
  353.8 1.3 copy-start.20
  354.3 1.1 copy-start.6
  356.0 0.8 copy-start.39
  356.8 0.8 copy-start.40
  475.2 5.9 copy-start.11
  475.3 5.9 copy-start.15
  475.3 5.9 copy-start.26
  475.3 5.9 copy-start.29
  475.6 6.7 collective-permute-start.8
  477.0 6.1 collective-permute-start.9
  481.8 1.3 copy-start.18
  481.8 1.3 copy-start.21
  482.3 1.1 copy-start.7
  484.0 0.8 copy-start.38
  484.0 1.4 copy-start.8
  485.4 0.8 copy-start.30
  601.9 1.8 copy-start.4
  601.9 1.8 copy-start.44
  603.8 1.0 copy-start.43
  609.5 220.5 %copy-start.47 = (f32[128,256]{1,0:T(8,128)S(1)}, f32[128,256]{1,0:T(8,128)}, u32[]{:S(2)}) copy-start(f32[128,256]{1,0:T(8,128)} %param.17) | copy-start | bytes 393220
  609.5 220.6 %copy-start.48 = (f32[256]{0:T(256)S(1)}, f32[256]{0:T(256)}, u32[]{:S(2)}) copy-start(f32[256]{0:T(256)} %param.15) | copy-start | bytes 3076
  650.0 180.9 %copy-start.23 = (f32[16,2,4,16,128]{4,3,2,1,0:T(8,128)S(1)}, f32[16,2,4,16,128]{4,3,2,1,0:T(8,128)}, u32[]{:S(2)}) copy-start(f32[16,2,4,16,128]{4,3,2,1,0:T(8,128)} %copy-done.22) | copy-start | bytes 3145732
  838.0 1.3 copy-start.1
Sparse Core Ops, SparseCore 0:
  89.9 61.6 all-gather.1
